TPU v7x, 512 devices: a whole 4x8x8 slice. The times are simulated.
512 devices in a mesh: frame: 8 (over y), space: 32 (over z, x), dp: 2 (over core).
Axes of the slice: x: 4, y: 8, z: 8, core: 2. Of those that a mesh axis runs over, the one named last changes fastest.
Arguments:
- frames_in: bfloat16 [16, 4096, 768], P(('dp', 'frame'), 'space'), parts along dimension 0, may hold values from -6 to 6
- cotangent: bfloat16 [16, 4096, 768], P(('dp', 'frame'), 'space'), parts along dimension 0, may hold values from -6 to 6
- w_qkv_space: bfloat16 [768, 2304], P('space'), may hold values from -0.21875 to 0.21875
- w_out_space: bfloat16 [768, 768], P('space'), may hold values from -0.875 to 0.875
- w_qkv_time: bfloat16 [768, 2304], P('space'), may hold values from -0.21875 to 0.21875
- w_out_time: bfloat16 [768, 768], P('space'), may hold values from -0.21875 to 0.21875
- neighbours: int32 [32, 4], replicated, may hold values from 0 to 31, as said below
Outputs:
- frames_out: bfloat16 [16, 4096, 768], P(('dp', 'frame'), 'space'), parts along dimension 0
- grad_frames: bfloat16 [16, 4096, 768], P(('dp', 'frame'), 'space'), parts along dimension 0
There are 2 independent parts, one for each index of `dp`. A program takes and returns all parts, laid end to end along the dimension named above; an argument that names none is the same for every part. Nothing has to cross between parts.
Inputs may be any that keep to these rules, and one draw needn't show every extreme that they name: `neighbours`: row b lists block b first; every entry c satisfies |c - b| <= 1; entries may repeat, and a repeated entry counts once.
All inputs are finite; a program needn't handle non-finite values.
Results may differ from a plain program's by a relative error of at most 0.023.
Values may be sent and summed in bfloat16 or wider, within the bound.
No kernel may reach another device: no remote copies, remote signals or barrier semaphores. Data moves between devices by JAX's collectives and lax.ppermute only.
A program may use at most 64 MiB of HBM per device.

v0:
```python
import jax
import jax.numpy as jnp
from jax import lax
from jax.sharding import PartitionSpec as P

HEADS = 12
HD = 64
BLOCK = 128
EPS = 1e-06


def padded(cells, sides, width):
    for axis, dim in sides:
        count = lax.axis_size(axis)
        ends = count - 1
        head = lax.slice_in_dim(cells, 0, width, axis=dim)
        tail = lax.slice_in_dim(cells, cells.shape[dim] - width, cells.shape[dim], axis=dim)
        cells = jnp.concatenate(
            [
                lax.ppermute(tail, axis, [(i, (i + 1) % count) for i in range(ends)]),
                cells,
                lax.ppermute(head, axis, [((i + 1) % count, i) for i in range(ends)]),
            ],
            axis=dim,
        )
    return cells


def rms_norm(row_data):
    values = row_data.astype(jnp.float32)
    factor = lax.rsqrt(jnp.mean(values * values, axis=-1, keepdims=True) + EPS)
    return (values * factor).astype(jnp.bfloat16)


def rms_back(row_data, upstream):
    values = row_data.astype(jnp.float32)
    factor = lax.rsqrt(jnp.mean(values * values, axis=-1, keepdims=True) + EPS)
    inner_mean = jnp.mean(values * upstream, axis=-1, keepdims=True)
    return factor * upstream - values * factor**3 * inner_mean


def block_mask(neighbour_rows, first_id):
    block_count = neighbour_rows.shape[0]
    candidate = first_id + jnp.arange(3 * block_count, dtype=jnp.int32)
    matches = jnp.any(neighbour_rows[:, :, None] == candidate[None, None, :], axis=1)
    return jnp.repeat(jnp.repeat(matches, BLOCK, axis=0), BLOCK, axis=1)


def space_attend(queries, key_rows, value_rows, allowed):
    score_scale = HD ** (-0.5)
    query_count = queries.shape[0]
    key_count = key_rows.shape[0]
    output_list = []
    total_list = []
    for head_pair in range(HEADS // 2):
        start_col = head_pair * 2 * HD
        stop_col = start_col + 2 * HD
        query_part = queries[:, start_col:stop_col].reshape(query_count, 2, HD)
        key_part = key_rows[:, start_col:stop_col].reshape(key_count, 2, HD)
        value_part = value_rows[:, start_col:stop_col].reshape(key_count, 2, HD)
        scores = (
            jnp.einsum("sgh,tgh->gst", query_part, key_part, preferred_element_type=jnp.float32)
            * score_scale
        )
        exponent = jnp.where(allowed[None], jnp.exp(scores), 0.0)
        totals = jnp.sum(exponent, axis=-1)
        probability = (exponent / totals[:, :, None]).astype(jnp.bfloat16)
        combined = jnp.einsum(
            "gst,tgh->sgh", probability, value_part, preferred_element_type=jnp.float32
        )
        output_list.append(combined.astype(jnp.bfloat16).reshape(query_count, 2 * HD))
        total_list.append(totals)
    return (jnp.concatenate(output_list, axis=1), jnp.concatenate(total_list, axis=0))


def space_back(queries, key_rows, value_rows, allowed, totals, attended, grad_attended):
    score_scale = HD ** (-0.5)
    query_count = queries.shape[0]
    key_count = key_rows.shape[0]
    query_list = []
    key_list = []
    value_list = []
    for head_pair in range(HEADS // 2):
        start_col = head_pair * 2 * HD
        stop_col = start_col + 2 * HD
        query_part = queries[:, start_col:stop_col].reshape(query_count, 2, HD)
        key_part = key_rows[:, start_col:stop_col].reshape(key_count, 2, HD)
        value_part = value_rows[:, start_col:stop_col].reshape(key_count, 2, HD)
        out_part = attended[:, start_col:stop_col].reshape(query_count, 2, HD)
        grad_part = grad_attended[:, start_col:stop_col].reshape(query_count, 2, HD)
        scores = (
            jnp.einsum("sgh,tgh->gst", query_part, key_part, preferred_element_type=jnp.float32)
            * score_scale
        )
        exponent = jnp.where(allowed[None], jnp.exp(scores), 0.0)
        weight = exponent / totals[2 * head_pair : 2 * head_pair + 2, :, None]
        probability = weight.astype(jnp.bfloat16)
        prob_grad = jnp.einsum(
            "sgh,tgh->gst", grad_part, value_part, preferred_element_type=jnp.float32
        )
        row_delta = jnp.einsum(
            "sgh,sgh->gs", grad_part, out_part, preferred_element_type=jnp.float32
        )
        score_grad = (weight * (prob_grad - row_delta[:, :, None])).astype(jnp.bfloat16)
        query_grad = (
            jnp.einsum("gst,tgh->sgh", score_grad, key_part, preferred_element_type=jnp.float32)
            * score_scale
        )
        key_grad = (
            jnp.einsum("gst,sgh->tgh", score_grad, query_part, preferred_element_type=jnp.float32)
            * score_scale
        )
        value_grad = jnp.einsum(
            "gst,sgh->tgh", probability, grad_part, preferred_element_type=jnp.float32
        )
        query_list.append(query_grad.astype(jnp.bfloat16).reshape(query_count, 2 * HD))
        key_list.append(key_grad.reshape(key_count, 2 * HD))
        value_list.append(value_grad.reshape(key_count, 2 * HD))
    return (
        jnp.concatenate(query_list, axis=1),
        jnp.concatenate(key_list, axis=1),
        jnp.concatenate(value_list, axis=1),
    )


def time_attend(queries, key_rows, value_rows):
    frame_count, position_count, feature_count = queries.shape
    split_shape = (frame_count, position_count, HEADS, HD)
    score_scale = HD ** (-0.5)
    scores = (
        jnp.einsum(
            "fphd,gphd->phfg",
            queries.reshape(split_shape),
            key_rows.reshape(split_shape),
            preferred_element_type=jnp.float32,
        )
        * score_scale
    )
    causal = jnp.arange(frame_count)[:, None] >= jnp.arange(frame_count)[None, :]
    exponent = jnp.where(causal, jnp.exp(scores), 0.0)
    totals = jnp.sum(exponent, axis=-1)
    probability = (exponent / totals[..., None]).astype(jnp.bfloat16)
    combined = jnp.einsum(
        "phfg,gphd->fphd",
        probability,
        value_rows.reshape(split_shape),
        preferred_element_type=jnp.float32,
    )
    return (
        combined.astype(jnp.bfloat16).reshape(frame_count, position_count, feature_count),
        totals,
    )


def time_back(queries, key_rows, value_rows, attended, grad_attended, totals):
    frame_count, position_count, feature_count = queries.shape
    split_shape = (frame_count, position_count, HEADS, HD)
    score_scale = HD ** (-0.5)
    query_four = queries.reshape(split_shape)
    key_four = key_rows.reshape(split_shape)
    value_four = value_rows.reshape(split_shape)
    out_four = attended.reshape(split_shape)
    grad_four = grad_attended.reshape(split_shape)
    scores = (
        jnp.einsum("fphd,gphd->phfg", query_four, key_four, preferred_element_type=jnp.float32)
        * score_scale
    )
    causal = jnp.arange(frame_count)[:, None] >= jnp.arange(frame_count)[None, :]
    exponent = jnp.where(causal, jnp.exp(scores), 0.0)
    weight = exponent / totals[..., None]
    probability = weight.astype(jnp.bfloat16)
    prob_grad = jnp.einsum(
        "fphd,gphd->phfg", grad_four, value_four, preferred_element_type=jnp.float32
    )
    row_delta = jnp.einsum(
        "fphd,fphd->phf", grad_four, out_four, preferred_element_type=jnp.float32
    )
    score_grad = (weight * (prob_grad - row_delta[..., None])).astype(jnp.bfloat16)
    query_grad = (
        jnp.einsum("phfg,gphd->fphd", score_grad, key_four, preferred_element_type=jnp.float32)
        * score_scale
    )
    key_grad = (
        jnp.einsum("phfg,fphd->gphd", score_grad, query_four, preferred_element_type=jnp.float32)
        * score_scale
    )
    value_grad = jnp.einsum(
        "phfg,fphd->gphd", probability, grad_four, preferred_element_type=jnp.float32
    )
    pieces = [
        gradient.astype(jnp.bfloat16).reshape(frame_count, position_count, feature_count)
        for gradient in (query_grad, key_grad, value_grad)
    ]
    return jnp.concatenate(pieces, axis=-1)


def to_frames(local_rows):
    return lax.all_to_all(local_rows[None], "frame", split_axis=1, concat_axis=0, tiled=True)


def to_space(frame_rows):
    return lax.all_to_all(frame_rows, "frame", split_axis=0, concat_axis=1, tiled=True)[0]


def rim(first_part, second_part, width):
    return (padded(first_part, (("space", 0),), width), padded(second_part, (("space", 0),), width))


def local(frames_in, cotangent, w_qkv_space, w_out_space, w_qkv_time, w_out_time, neighbours):
    local_in = frames_in[0]
    grad_out = cotangent[0]
    shard, feature_count = local_in.shape
    full_qkv_space, full_out_space, full_qkv_time, full_out_time = (
        lax.all_gather(w_qkv_space, "space", axis=0, tiled=True),
        lax.all_gather(w_out_space, "space", axis=0, tiled=True),
        lax.all_gather(w_qkv_time, "space", axis=0, tiled=True),
        lax.all_gather(w_out_time, "space", axis=0, tiled=True),
    )
    block_count = shard // BLOCK
    space_index = lax.axis_index("space")
    lists_here = lax.dynamic_slice_in_dim(neighbours, space_index * block_count, block_count, 0)
    allowed = block_mask(lists_here, (space_index - 1) * block_count)
    normed_space = rms_norm(local_in)
    projected = jnp.dot(normed_space, full_qkv_space, preferred_element_type=jnp.float32).astype(
        jnp.bfloat16
    )
    queries = projected[:, :feature_count]
    key_window, value_window = rim(
        projected[:, feature_count : 2 * feature_count], projected[:, 2 * feature_count :], shard
    )
    attended, totals = space_attend(queries, key_window, value_window, allowed)
    update = jnp.dot(attended, full_out_space, preferred_element_type=jnp.float32)
    stream = (local_in.astype(jnp.float32) + update).astype(jnp.bfloat16)
    normed_time = rms_norm(stream)
    projected_time = jnp.dot(normed_time, full_qkv_time, preferred_element_type=jnp.float32).astype(
        jnp.bfloat16
    )
    time_rows = to_frames(projected_time)
    query_time = time_rows[..., :feature_count]
    key_time = time_rows[..., feature_count : 2 * feature_count]
    value_time = time_rows[..., 2 * feature_count :]
    attended_time, totals_time = time_attend(query_time, key_time, value_time)
    attended_back = to_space(attended_time)
    update_time = jnp.dot(attended_back, full_out_time, preferred_element_type=jnp.float32)
    frames_out = (stream.astype(jnp.float32) + update_time).astype(jnp.bfloat16)
    grad_att_time = jnp.dot(grad_out, full_out_time.T, preferred_element_type=jnp.float32).astype(
        jnp.bfloat16
    )
    grad_time_rows = to_frames(grad_att_time)
    gradients = time_back(
        query_time, key_time, value_time, attended_time, grad_time_rows, totals_time
    )
    grad_project_time = to_space(gradients)
    grad_normed_time = jnp.dot(
        grad_project_time, full_qkv_time.T, preferred_element_type=jnp.float32
    )
    grad_stream = (grad_out.astype(jnp.float32) + rms_back(stream, grad_normed_time)).astype(
        jnp.bfloat16
    )
    grad_attended = jnp.dot(
        grad_stream, full_out_space.T, preferred_element_type=jnp.float32
    ).astype(jnp.bfloat16)
    grad_query, key_partial, value_partial = space_back(
        queries, key_window, value_window, allowed, totals, attended, grad_attended
    )
    key_send = jnp.concatenate([key_partial[:shard], key_partial[2 * shard :]], axis=0).astype(
        jnp.bfloat16
    )
    value_send = jnp.concatenate(
        [value_partial[:shard], value_partial[2 * shard :]], axis=0
    ).astype(jnp.bfloat16)
    key_got, value_got = rim(key_send, value_send, shard)
    grad_key = (
        key_partial[shard : 2 * shard]
        + key_got[:shard].astype(jnp.float32)
        + key_got[3 * shard :].astype(jnp.float32)
    ).astype(jnp.bfloat16)
    grad_value = (
        value_partial[shard : 2 * shard]
        + value_got[:shard].astype(jnp.float32)
        + value_got[3 * shard :].astype(jnp.float32)
    ).astype(jnp.bfloat16)
    grad_project = jnp.concatenate([grad_query, grad_key, grad_value], axis=1)
    grad_normed = jnp.dot(grad_project, full_qkv_space.T, preferred_element_type=jnp.float32)
    grad_in = (grad_stream.astype(jnp.float32) + rms_back(local_in, grad_normed)).astype(
        jnp.bfloat16
    )
    return (frames_out[None], grad_in[None])


def solution(mesh):
    in_specs = (
        P(("dp", "frame"), "space", None),
        P(("dp", "frame"), "space", None),
        P("space", None),
        P("space", None),
        P("space", None),
        P("space", None),
        P(),
    )
    out_specs = (P(("dp", "frame"), "space", None), P(("dp", "frame"), "space", None))
    return jax.shard_map(local, mesh=mesh, in_specs=in_specs, out_specs=out_specs, check_vma=False)
```

profile of v0, /device:TPU:64, one launch (start us, length us, event | category | flops | bytes accessed | tf_op | source)
XLA Modules:
  0.0 482.6 jit_solution(3111090518492652607)
XLA Ops:
  12.0 84.9 %all-gather.11.cloned.1.call-done = bf16[768,768]{1,0:T(8,128)(2,1)} async-done(((bf16[24,768]{1,0:T(8,128)(2,1)}), bf16[768,768]{1,0:T(8,128)(2,1)}) %all-gather.11.cloned.1.call-update) | async-done | bytes 1179664 | tf_op jit(solution)/shard_map/all_gather | solution.py:217
  102.2 6.7 %all-to-all-start.2 = ((bf16[8,2,6144]{2,1,0:T(2,128)(2,1)}), bf16[8,2,6144]{2,1,0:T(2,128)(2,1)S(1)}, u32[]{:S(2)}, u32[]{:S(2)}) async-start(bf16[8,2,6144]{2,1,0:T(2,128)(2,1)} %reshape.405), calls=%async_computation.2 | async-start | bytes 393216 | tf_op jit(solution)/shard_map/all_to_all | solution.py:198
  108.9 75.4 %all-gather.5.cloned.1.call-done = bf16[768,2304]{1,0:T(8,128)(2,1)} async-done(((bf16[24,2304]{1,0:T(8,128)(2,1)}), bf16[768,2304]{1,0:T(8,128)(2,1)}) %all-gather.5.cloned.1.call-update) | async-done | bytes 3538960 | tf_op jit(solution)/shard_map/all_gather | solution.py:214
  184.4 2.7 convolution_convert_fusion.1
  187.1 3.6 collective-permute-start.1
  192.9 5.7 %collective-permute-start.3 = (bf16[128,768]{1,0:T(8,128)(2,1)S(1)}, bf16[128,768]{1,0:T(8,128)(2,1)S(1)}, u32[]{:S(2)}, u32[]{:S(2)}) collective-permute-start(bf16[128,768]{1,0:T(8,128)(2,1)S(1)} %get-tuple-element.27), channel_id=1, source_target_pairs={{2,0},{4,2},{6,4},{8,6},{10,8},{12,10},{14,12},{16,14},{18,16},{20... | collective-permute-start | bytes 589832 | tf_op jit(solution)/shard_map/ppermute | solution.py:22
  202.0 6.4 %collective-permute-done.2 = bf16[128,768]{1,0:T(8,128)(2,1)S(1)} collective-permute-done((bf16[128,768]{1,0:T(8,128)(2,1)S(1)}, bf16[128,768]{1,0:T(8,128)(2,1)S(1)}, u32[]{:S(2)}, u32[]{:S(2)}) %collective-permute-start.2) | collective-permute-done | bytes 196640 | tf_op jit(solution)/shard_map/ppermute | solution.py:20
  214.0 52.5 %all-gather.7.cloned.1.call-done = bf16[768,768]{1,0:T(8,128)(2,1)} async-done(((bf16[24,768]{1,0:T(8,128)(2,1)}), bf16[768,768]{1,0:T(8,128)(2,1)}) %all-gather.7.cloned.1.call-update) | async-done | bytes 1179664 | tf_op jit(solution)/shard_map/all_gather | solution.py:215
  268.8 85.1 %all-gather.9.cloned.1.call-done = bf16[768,2304]{1,0:T(8,128)(2,1)} async-done(((bf16[24,2304]{1,0:T(8,128)(2,1)}), bf16[768,2304]{1,0:T(8,128)(2,1)}) %all-gather.9.cloned.1.call-update) | async-done | bytes 3538960 | tf_op jit(solution)/shard_map/all_gather | solution.py:216
  353.9 2.7 fusion
  357.5 4.4 reduce.20
  362.8 6.7 %all-to-all-start = ((bf16[8,2,18432]{2,1,0:T(2,128)(2,1)}), bf16[8,2,18432]{2,1,0:T(2,128)(2,1)S(1)}, u32[]{:S(2)}, u32[]{:S(2)}) async-start(bf16[8,2,18432]{2,1,0:T(2,128)(2,1)} %reshape.403), calls=%async_computation | async-start | bytes 1179648 | tf_op jit(solution)/shard_map/all_to_all | solution.py:198
  374.6 10.4 %all-to-all-done = bf16[8,2,18432]{2,1,0:T(2,128)(2,1)S(1)} async-done(((bf16[8,2,18432]{2,1,0:T(2,128)(2,1)}), bf16[8,2,18432]{2,1,0:T(2,128)(2,1)S(1)}, u32[]{:S(2)}, u32[]{:S(2)}) %all-to-all-start) | async-done | bytes 589856 | tf_op jit(solution)/shard_map/all_to_all | solution.py:198
  388.5 2.7 fusion.7
  391.2 2.5 fusion.57
  395.0 3.1 multiply_reduce_fusion
  401.8 3.4 all-to-all-start.1
  407.4 7.5 %all-to-all-done.1 = bf16[8,16,768]{2,1,0:T(8,128)(2,1)S(1)} async-done(((bf16[8,16,768]{2,1,0:T(8,128)(2,1)}), bf16[8,16,768]{2,1,0:T(8,128)(2,1)S(1)}, u32[]{:S(2)}, u32[]{:S(2)}) %all-to-all-start.1) | async-done | bytes 196640 | tf_op jit(solution)/shard_map/all_to_all | solution.py:202
  414.9 4.5 all-to-all-start.3
  427.3 5.8 %all-to-all-done.3 = bf16[8,16,2304]{2,1,0:T(8,128)(2,1)} async-done(((bf16[8,16,2304]{2,1,0:T(8,128)(2,1)}), bf16[8,16,2304]{2,1,0:T(8,128)(2,1)}, u32[]{:S(2)}, u32[]{:S(2)}) %all-to-all-start.3) | async-done | bytes 589856 | tf_op jit(solution)/shard_map/all_to_all | solution.py:202
  433.1 2.6 multiply_reduce_fusion.1
  451.8 3.6 collective-permute-start.5
  458.0 6.0 %collective-permute-start.7 = (bf16[128,768]{0,1:T(8,128)(2,1)S(1)}, bf16[128,768]{0,1:T(8,128)(2,1)S(1)}, u32[]{:S(2)}, u32[]{:S(2)}) collective-permute-start(bf16[128,768]{0,1:T(8,128)(2,1)S(1)} %get-tuple-element.3), channel_id=1, source_target_pairs={{2,0},{4,2},{6,4},{8,6},{10,8},{12,10},{14,12},{16,14},{18,16},{20... | collective-permute-start | bytes 589832 | tf_op jit(solution)/shard_map/ppermute | solution.py:22
  467.1 6.5 %collective-permute-done.6 = bf16[128,768]{0,1:T(8,128)(2,1)S(1)} collective-permute-done((bf16[128,768]{0,1:T(8,128)(2,1)S(1)}, bf16[128,768]{0,1:T(8,128)(2,1)S(1)}, u32[]{:S(2)}, u32[]{:S(2)}) %collective-permute-start.6) | collective-permute-done | bytes 196640 | tf_op jit(solution)/shard_map/ppermute | solution.py:20
  (340 shorter events, 71.4 us)
Async XLA Ops:
  7.2 89.7 %all-gather.11.cloned.1.call-start = ((), (), s32[]{:S(2)}) async-start(), calls=%async_computation.7 | async-start | bytes 1216512 | tf_op jit(solution)/shard_map/all_gather | solution.py:217
  7.9 176.4 %all-gather.5.cloned.1.call-start = ((), (), s32[]{:S(2)}) async-start(), calls=%async_computation.4 | async-start | bytes 3649536 | tf_op jit(solution)/shard_map/all_gather | solution.py:214
  8.7 257.8 %all-gather.7.cloned.1.call-start = ((), (), s32[]{:S(2)}) async-start(), calls=%async_computation.5 | async-start | bytes 1216512 | tf_op jit(solution)/shard_map/all_gather | solution.py:215
  9.4 344.5 %all-gather.9.cloned.1.call-start = ((), (), s32[]{:S(2)}) async-start(), calls=%async_computation.6 | async-start | bytes 3649536 | tf_op jit(solution)/shard_map/all_gather | solution.py:216
  98.8 85.6 %copy-start.5 = (bf16[1,128,768]{2,1,0:T(8,128)(2,1)S(1)}, bf16[1,128,768]{2,1,0:T(8,128)(2,1)}, u32[]{:S(2)}) copy-start(bf16[1,128,768]{2,1,0:T(8,128)(2,1)} %param.7) | copy-start | bytes 589828
  102.2 260.6 %all-to-all-start.2 = ((bf16[8,2,6144]{2,1,0:T(2,128)(2,1)}), bf16[8,2,6144]{2,1,0:T(2,128)(2,1)S(1)}, u32[]{:S(2)}, u32[]{:S(2)}) async-start(bf16[8,2,6144]{2,1,0:T(2,128)(2,1)} %reshape.405), calls=%async_computation.2 | async-start | bytes 393216 | tf_op jit(solution)/shard_map/all_to_all | solution.py:198
  187.1 14.5 %collective-permute-start.1 = (bf16[128,768]{1,0:T(8,128)(2,1)S(1)}, bf16[128,768]{1,0:T(8,128)(2,1)S(1)}, u32[]{:S(2)}, u32[]{:S(2)}) collective-permute-start(bf16[128,768]{1,0:T(8,128)(2,1)S(1)} %get-tuple-element.28), channel_id=1, source_target_pairs={{2,0},{4,2},{6,4},{8,6},{10,8},{12,10},{14,12},{16,14},{18,16},{20... | collective-permute-start | bytes 589832 | tf_op jit(solution)/shard_map/ppermute | solution.py:22
  190.7 10.9 %collective-permute-start = (bf16[128,768]{1,0:T(8,128)(2,1)S(1)}, bf16[128,768]{1,0:T(8,128)(2,1)S(1)}, u32[]{:S(2)}, u32[]{:S(2)}) collective-permute-start(bf16[128,768]{1,0:T(8,128)(2,1)S(1)} %get-tuple-element.28), channel_id=1, source_target_pairs={{0,2},{2,4},{4,6},{6,8},{8,10},{10,12},{12,14},{14,16},{16,18},{18... | collective-permute-start | bytes 589832 | tf_op jit(solution)/shard_map/ppermute | solution.py:20
  192.9 9.1 %collective-permute-start.3 = (bf16[128,768]{1,0:T(8,128)(2,1)S(1)}, bf16[128,768]{1,0:T(8,128)(2,1)S(1)}, u32[]{:S(2)}, u32[]{:S(2)}) collective-permute-start(bf16[128,768]{1,0:T(8,128)(2,1)S(1)} %get-tuple-element.27), channel_id=1, source_target_pairs={{2,0},{4,2},{6,4},{8,6},{10,8},{12,10},{14,12},{16,14},{18,16},{20... | collective-permute-start | bytes 589832 | tf_op jit(solution)/shard_map/ppermute | solution.py:22
  198.7 9.8 %collective-permute-start.2 = (bf16[128,768]{1,0:T(8,128)(2,1)S(1)}, bf16[128,768]{1,0:T(8,128)(2,1)S(1)}, u32[]{:S(2)}, u32[]{:S(2)}) collective-permute-start(bf16[128,768]{1,0:T(8,128)(2,1)S(1)} %get-tuple-element.27), channel_id=1, source_target_pairs={{0,2},{2,4},{4,6},{6,8},{8,10},{10,12},{12,14},{14,16},{16,18},{18... | collective-permute-start | bytes 589832 | tf_op jit(solution)/shard_map/ppermute | solution.py:20
  209.6 211.0 %copy-start.12 = (bf16[384,128]{0,1:T(8,128)(2,1)}, bf16[384,128]{0,1:T(8,128)(2,1)S(1)}, u32[]{:S(2)}) copy-start(bf16[384,128]{0,1:T(8,128)(2,1)S(1)} %copy.194) | copy-start | bytes 294916
  209.8 211.8 %copy-start.10 = (bf16[384,128]{0,1:T(8,128)(2,1)}, bf16[384,128]{0,1:T(8,128)(2,1)S(1)}, u32[]{:S(2)}) copy-start(bf16[384,128]{0,1:T(8,128)(2,1)S(1)} %copy.197) | copy-start | bytes 294916
  213.3 54.9 %copy-start.70 = (bf16[2,64,128]{2,1,0:T(8,128)(2,1)}, bf16[2,64,128]{2,1,0:T(8,128)(2,1)S(1)}, u32[]{:S(2)}) copy-start(bf16[2,64,128]{2,1,0:T(8,128)(2,1)S(1)} %convolution_convert_fusion.7) | copy-start | bytes 98308
  213.7 54.6 %copy-start.32 = (f32[2,128,384]{2,1,0:T(8,128)}, f32[2,128,384]{2,1,0:T(8,128)S(1)}, u32[]{:S(2)}) copy-start(f32[2,128,384]{2,1,0:T(8,128)S(1)} %fusion.21) | copy-start | bytes 1179652
  214.0 142.6 %copy-start.68 = (bf16[2,64,128]{2,1,0:T(8,128)(2,1)}, bf16[2,64,128]{2,1,0:T(8,128)(2,1)S(1)}, u32[]{:S(2)}) copy-start(bf16[2,64,128]{2,1,0:T(8,128)(2,1)S(1)} %convolution_convert_fusion.6) | copy-start | bytes 98308
  268.3 88.3 %copy-start.3 = (f32[128,768]{1,0:T(8,128)}, f32[128,768]{1,0:T(8,128)S(1)}, u32[]{:S(2)}) copy-start(f32[128,768]{1,0:T(8,128)S(1)} %get-tuple-element.40) | copy-start | bytes 1179652
  362.8 22.1 %all-to-all-start = ((bf16[8,2,18432]{2,1,0:T(2,128)(2,1)}), bf16[8,2,18432]{2,1,0:T(2,128)(2,1)S(1)}, u32[]{:S(2)}, u32[]{:S(2)}) async-start(bf16[8,2,18432]{2,1,0:T(2,128)(2,1)} %reshape.403), calls=%async_computation | async-start | bytes 1179648 | tf_op jit(solution)/shard_map/all_to_all | solution.py:198
  401.8 13.1 %all-to-all-start.1 = ((bf16[8,16,768]{2,1,0:T(8,128)(2,1)}), bf16[8,16,768]{2,1,0:T(8,128)(2,1)S(1)}, u32[]{:S(2)}, u32[]{:S(2)}) async-start(bf16[8,16,768]{2,1,0:T(8,128)(2,1)} %reshape.350), calls=%async_computation.1 | async-start | bytes 393216 | tf_op jit(solution)/shard_map/all_to_all | solution.py:202
  414.9 18.2 %all-to-all-start.3 = ((bf16[8,16,2304]{2,1,0:T(8,128)(2,1)}), bf16[8,16,2304]{2,1,0:T(8,128)(2,1)}, u32[]{:S(2)}, u32[]{:S(2)}) async-start(bf16[8,16,2304]{2,1,0:T(8,128)(2,1)} %pad_maximum_fusion.2), calls=%async_computation.3 | async-start | bytes 1179648 | tf_op jit(solution)/shard_map/all_to_all | solution.py:202
  451.8 14.2 %collective-permute-start.5 = (bf16[128,768]{0,1:T(8,128)(2,1)S(1)}, bf16[128,768]{0,1:T(8,128)(2,1)S(1)}, u32[]{:S(2)}, u32[]{:S(2)}) collective-permute-start(bf16[128,768]{0,1:T(8,128)(2,1)S(1)} %get-tuple-element.5), channel_id=1, source_target_pairs={{2,0},{4,2},{6,4},{8,6},{10,8},{12,10},{14,12},{16,14},{18,16},{20... | collective-permute-start | bytes 589832 | tf_op jit(solution)/shard_map/ppermute | solution.py:22
  455.5 10.8 %collective-permute-start.4 = (bf16[128,768]{0,1:T(8,128)(2,1)S(1)}, bf16[128,768]{0,1:T(8,128)(2,1)S(1)}, u32[]{:S(2)}, u32[]{:S(2)}) collective-permute-start(bf16[128,768]{0,1:T(8,128)(2,1)S(1)} %get-tuple-element.4), channel_id=1, source_target_pairs={{0,2},{2,4},{4,6},{6,8},{8,10},{10,12},{12,14},{14,16},{16,18},{18... | collective-permute-start | bytes 589832 | tf_op jit(solution)/shard_map/ppermute | solution.py:20
  457.8 15.9 %copy-start.1 = (bf16[768,2304]{1,0:T(8,128)(2,1)S(1)}, bf16[768,2304]{1,0:T(8,128)(2,1)}, u32[]{:S(2)}) copy-start(bf16[768,2304]{1,0:T(8,128)(2,1)} %all-gather.5.cloned.1.call-done) | copy-start | bytes 10616836
  458.0 9.2 %collective-permute-start.7 = (bf16[128,768]{0,1:T(8,128)(2,1)S(1)}, bf16[128,768]{0,1:T(8,128)(2,1)S(1)}, u32[]{:S(2)}, u32[]{:S(2)}) collective-permute-start(bf16[128,768]{0,1:T(8,128)(2,1)S(1)} %get-tuple-element.3), channel_id=1, source_target_pairs={{2,0},{4,2},{6,4},{8,6},{10,8},{12,10},{14,12},{16,14},{18,16},{20... | collective-permute-start | bytes 589832 | tf_op jit(solution)/shard_map/ppermute | solution.py:22
  464.0 9.7 %collective-permute-start.6 = (bf16[128,768]{0,1:T(8,128)(2,1)S(1)}, bf16[128,768]{0,1:T(8,128)(2,1)S(1)}, u32[]{:S(2)}, u32[]{:S(2)}) collective-permute-start(bf16[128,768]{0,1:T(8,128)(2,1)S(1)} %get-tuple-element.2), channel_id=1, source_target_pairs={{0,2},{2,4},{4,6},{6,8},{8,10},{10,12},{12,14},{14,16},{16,18},{18... | collective-permute-start | bytes 589832 | tf_op jit(solution)/shard_map/ppermute | solution.py:20
  (75 other events, 227.9 us)
Sparse Core Ops, SparseCore 0:
  11.2 85.5 all-gather.10
  100.0 84.2 all-gather.4
  187.6 78.8 all-gather.6
  269.5 84.2 all-gather.8
where the time goes:
time: 484 us; the launch traced here: 483 us
  waiting for transfers between devices  338 us (70%)
  starting transfers between devices  48.9 us (10%)
  matrix products  48.9 us (10%)
  local copies, waits for them, and re-layouts  16.5 us (3%)
  between operations  15.8 us (3%)
  other arithmetic  14.1 us (3%)
    all_gather x1, waiting for transfers between devices, local(): lax.all_gather(w_qkv_time, 'space', axis=0, tiled=True)  85.1 us
    all_gather x1, waiting for transfers between devices, local(): lax.all_gather(w_out_time, 'space', axis=0, tiled=True)  84.9 us
    all_gather x1, waiting for transfers between devices, local(): lax.all_gather(w_qkv_space, 'space', axis=0, tiled=True)  75.4 us
    all_gather x1, waiting for transfers between devices, local(): lax.all_gather(w_out_space, 'space', axis=0, tiled=True)  52.5 us
    ppermute x4, starting transfers between devices, padded(): lax.ppermute(head, axis, [((i + 1) % count, i) for i in range(ends)])  19 us
    all_to_all x2, starting transfers between devices, to_frames(): lax.all_to_all(local_rows[None], 'frame', split_axis=1, concat_axis=0, ti...  13.5 us
    all_to_all x2, waiting for transfers between devices, to_space(): lax.all_to_all(frame_rows, 'frame', split_axis=0, concat_axis=1, tiled=True)  13.3 us
    ppermute x4, waiting for transfers between devices, padded(): lax.ppermute(tail, axis, [(i, (i + 1) % count) for i in range(ends)])  13.2 us
  transfers between devices with their start and end apart: 16, of which 12 were waited for; matrix products, arithmetic and copies ran while one was open for 9% of the time, Pallas kernels for 0%

commit v1 on v0

--- a/solution.py
+++ b/solution.py
@@ -7,6 +7,11 @@
 HD = 64
 BLOCK = 128
 EPS = 1e-06
+
+
+def gather_from_all(shard, axis, dim):
+    copies = jnp.concatenate([shard] * lax.axis_size(axis), axis=dim)
+    return lax.all_to_all(copies, axis, dim, dim, tiled=True)
 
 
 def padded(cells, sides, width):
@@ -214,7 +219,7 @@
         lax.all_gather(w_qkv_space, "space", axis=0, tiled=True),
         lax.all_gather(w_out_space, "space", axis=0, tiled=True),
         lax.all_gather(w_qkv_time, "space", axis=0, tiled=True),
-        lax.all_gather(w_out_time, "space", axis=0, tiled=True),
+        gather_from_all(w_out_time, "space", 0),
     )
     block_count = shard // BLOCK
     space_index = lax.axis_index("space")

time: 484 us -> 406 us (0.84)
  waiting for transfers between devices: 338 us -> 218 us
  local copies, waits for them, and re-layouts: 16.5 us -> 46.2 us
  starting transfers between devices: 48.9 us -> 63.1 us
    all_gather x1 -> x0, waiting for transfers between devices: 84.9 us -> none  [local(): lax.all_gather(w_out_time, 'space', axis=0, tiled=True)]
    all_gather x1, waiting for transfers between devices: 75.4 us -> 8.31 us  [local(): lax.all_gather(w_qkv_space, 'space', axis=0, tiled=True)]
    all_to_all x0 -> x1, waiting for transfers between devices: none -> 31.3 us  [gather_from_all(): return lax.all_to_all(copies, axis, dim, dim, tiled=True)]
    unnamed x193 -> x226, local copies, waits for them, and re-layouts: 5.5 us -> 36 us
    all_to_all x0 -> x1, starting transfers between devices: none -> 12.7 us  [gather_from_all(): return lax.all_to_all(copies, axis, dim, dim, tiled=True)]
  transfers between devices with their start and end apart: 16 -> 16, of which waited for: 12 -> 11; matrix products, arithmetic and copies ran while one was open for 9% -> 17% of each run, Pallas kernels for 0% -> 0%
where the time goes in v1:
time: 406 us; the launch traced here: 404 us
  waiting for transfers between devices  218 us (54%)
  starting transfers between devices  63.1 us (16%)
  matrix products  47.5 us (12%)
  local copies, waits for them, and re-layouts  46.2 us (11%)
  between operations  15.8 us (4%)
  other arithmetic  13.2 us (3%)
    all_gather x1, waiting for transfers between devices, local(): lax.all_gather(w_qkv_time, 'space', axis=0, tiled=True)  85.2 us
    all_gather x1, waiting for transfers between devices, local(): lax.all_gather(w_out_space, 'space', axis=0, tiled=True)  53.3 us
    unnamed x226, local copies, waits for them, and re-layouts  36 us
    all_to_all x1, waiting for transfers between devices, gather_from_all(): return lax.all_to_all(copies, axis, dim, dim, tiled=True)  31.3 us
    ppermute x4, starting transfers between devices, padded(): lax.ppermute(head, axis, [((i + 1) % count, i) for i in range(ends)])  20.4 us
    all_to_all x2, starting transfers between devices, to_frames(): lax.all_to_all(local_rows[None], 'frame', split_axis=1, concat_axis=0, ti...  13.8 us
    all_to_all x2, waiting for transfers between devices, to_space(): lax.all_to_all(frame_rows, 'frame', split_axis=0, concat_axis=1, tiled=True)  13.3 us
    ppermute x4, waiting for transfers between devices, padded(): lax.ppermute(tail, axis, [(i, (i + 1) % count) for i in range(ends)])  13.2 us
  transfers between devices with their start and end apart: 16, of which 11 were waited for; matrix products, arithmetic and copies ran while one was open for 17% of the time, Pallas kernels for 0%

profile of v1, /device:TPU:64, one launch (start us, length us, event | category | flops | bytes accessed | tf_op | source)
XLA Modules:
  0.0 403.8 jit_solution(14815984744040046977)
XLA Ops:
  39.1 12.7 %all-to-all-start.2 = ((bf16[32,24,768]{2,1,0:T(8,128)(2,1)}), bf16[32,24,768]{2,1,0:T(8,128)(2,1)S(1)}, u32[]{:S(2)}, u32[]{:S(2)}) async-start(bf16[32,24,768]{2,1,0:T(8,128)(2,1)} %bitcast.50), calls=%async_computation.2 | async-start | bytes 2359296 | tf_op jit(solution)/shard_map/all_to_all | solution.py:14
  53.6 31.3 %all-to-all-done.2 = bf16[32,24,768]{2,1,0:T(8,128)(2,1)S(1)} async-done(((bf16[32,24,768]{2,1,0:T(8,128)(2,1)}), bf16[32,24,768]{2,1,0:T(8,128)(2,1)S(1)}, u32[]{:S(2)}, u32[]{:S(2)}) %all-to-all-start.2) | async-done | bytes 1179680 | tf_op jit(solution)/shard_map/all_to_all | solution.py:14
  89.0 7.0 %all-to-all-start.3 = ((bf16[8,2,6144]{2,1,0:T(2,128)(2,1)}), bf16[8,2,6144]{2,1,0:T(2,128)(2,1)S(1)}, u32[]{:S(2)}, u32[]{:S(2)}) async-start(bf16[8,2,6144]{2,1,0:T(2,128)(2,1)} %reshape.407), calls=%async_computation.3 | async-start | bytes 393216 | tf_op jit(solution)/shard_map/all_to_all | solution.py:203
  96.0 8.3 %all-gather.4.cloned.1.call-done = bf16[768,2304]{1,0:T(8,128)(2,1)} async-done(((bf16[24,2304]{1,0:T(8,128)(2,1)}), bf16[768,2304]{1,0:T(8,128)(2,1)}) %all-gather.4.cloned.1.call-update) | async-done | bytes 3538960 | tf_op jit(solution)/shard_map/all_gather | solution.py:219
  104.3 2.7 convolution_convert_fusion.1
  107.0 4.8 %collective-permute-start.1 = (bf16[128,768]{1,0:T(8,128)(2,1)S(1)}, bf16[128,768]{1,0:T(8,128)(2,1)S(1)}, u32[]{:S(2)}, u32[]{:S(2)}) collective-permute-start(bf16[128,768]{1,0:T(8,128)(2,1)S(1)} %get-tuple-element.28), channel_id=1, source_target_pairs={{2,0},{4,2},{6,4},{8,6},{10,8},{12,10},{14,12},{16,14},{18,16},{20... | collective-permute-start | bytes 589832 | tf_op jit(solution)/shard_map/ppermute | solution.py:27
  113.8 6.0 %collective-permute-start.3 = (bf16[128,768]{1,0:T(8,128)(2,1)S(1)}, bf16[128,768]{1,0:T(8,128)(2,1)S(1)}, u32[]{:S(2)}, u32[]{:S(2)}) collective-permute-start(bf16[128,768]{1,0:T(8,128)(2,1)S(1)} %get-tuple-element.27), channel_id=1, source_target_pairs={{2,0},{4,2},{6,4},{8,6},{10,8},{12,10},{14,12},{16,14},{18,16},{20... | collective-permute-start | bytes 589832 | tf_op jit(solution)/shard_map/ppermute | solution.py:27
  123.1 6.5 %collective-permute-done.2 = bf16[128,768]{1,0:T(8,128)(2,1)S(1)} collective-permute-done((bf16[128,768]{1,0:T(8,128)(2,1)S(1)}, bf16[128,768]{1,0:T(8,128)(2,1)S(1)}, u32[]{:S(2)}, u32[]{:S(2)}) %collective-permute-start.2) | collective-permute-done | bytes 196640 | tf_op jit(solution)/shard_map/ppermute | solution.py:25
  135.9 53.3 %all-gather.6.cloned.1.call-done = bf16[768,768]{1,0:T(8,128)(2,1)} async-done(((bf16[24,768]{1,0:T(8,128)(2,1)}), bf16[768,768]{1,0:T(8,128)(2,1)}) %all-gather.6.cloned.1.call-update) | async-done | bytes 1179664 | tf_op jit(solution)/shard_map/all_gather | solution.py:220
  191.5 85.2 %all-gather.8.cloned.1.call-done = bf16[768,2304]{1,0:T(8,128)(2,1)} async-done(((bf16[24,2304]{1,0:T(8,128)(2,1)}), bf16[768,2304]{1,0:T(8,128)(2,1)}) %all-gather.8.cloned.1.call-update) | async-done | bytes 3538960 | tf_op jit(solution)/shard_map/all_gather | solution.py:221
  276.7 2.7 fusion
  280.3 4.4 %reduce.20 = bf16[128,2304]{1,0:T(8,128)(2,1)S(1)} reduce(bf16[128,1,2304]{2,1,0:T(2,128)(2,1)S(1)} %bitcast.298, bf16[]{:T(256)} %broadcast.211), dimensions={1}, to_apply=%bitcast.295.reduce_sub_computation | reduce | bytes 1179650
  285.7 6.7 %all-to-all-start = ((bf16[8,2,18432]{2,1,0:T(2,128)(2,1)}), bf16[8,2,18432]{2,1,0:T(2,128)(2,1)S(1)}, u32[]{:S(2)}, u32[]{:S(2)}) async-start(bf16[8,2,18432]{2,1,0:T(2,128)(2,1)} %reshape.405), calls=%async_computation | async-start | bytes 1179648 | tf_op jit(solution)/shard_map/all_to_all | solution.py:203
  297.3 10.5 %all-to-all-done = bf16[8,2,18432]{2,1,0:T(2,128)(2,1)S(1)} async-done(((bf16[8,2,18432]{2,1,0:T(2,128)(2,1)}), bf16[8,2,18432]{2,1,0:T(2,128)(2,1)S(1)}, u32[]{:S(2)}, u32[]{:S(2)}) %all-to-all-start) | async-done | bytes 589856 | tf_op jit(solution)/shard_map/all_to_all | solution.py:203
  310.7 2.7 fusion.7
  316.2 3.1 multiply_reduce_fusion
  323.1 3.4 all-to-all-start.1
  328.6 7.5 %all-to-all-done.1 = bf16[8,16,768]{2,1,0:T(8,128)(2,1)S(1)} async-done(((bf16[8,16,768]{2,1,0:T(8,128)(2,1)}), bf16[8,16,768]{2,1,0:T(8,128)(2,1)S(1)}, u32[]{:S(2)}, u32[]{:S(2)}) %all-to-all-start.1) | async-done | bytes 196640 | tf_op jit(solution)/shard_map/all_to_all | solution.py:207
  336.2 4.5 %all-to-all-start.4 = ((bf16[8,16,2304]{2,1,0:T(8,128)(2,1)}), bf16[8,16,2304]{2,1,0:T(8,128)(2,1)}, u32[]{:S(2)}, u32[]{:S(2)}) async-start(bf16[8,16,2304]{2,1,0:T(8,128)(2,1)} %pad_maximum_fusion.2), calls=%async_computation.4 | async-start | bytes 1179648 | tf_op jit(solution)/shard_map/all_to_all | solution.py:207
  348.6 5.8 %all-to-all-done.4 = bf16[8,16,2304]{2,1,0:T(8,128)(2,1)} async-done(((bf16[8,16,2304]{2,1,0:T(8,128)(2,1)}), bf16[8,16,2304]{2,1,0:T(8,128)(2,1)}, u32[]{:S(2)}, u32[]{:S(2)}) %all-to-all-start.4) | async-done | bytes 589856 | tf_op jit(solution)/shard_map/all_to_all | solution.py:207
  354.4 2.6 multiply_reduce_fusion.1
  373.1 3.6 collective-permute-start.5
  379.2 6.0 %collective-permute-start.7 = (bf16[128,768]{0,1:T(8,128)(2,1)S(1)}, bf16[128,768]{0,1:T(8,128)(2,1)S(1)}, u32[]{:S(2)}, u32[]{:S(2)}) collective-permute-start(bf16[128,768]{0,1:T(8,128)(2,1)S(1)} %get-tuple-element.3), channel_id=1, source_target_pairs={{2,0},{4,2},{6,4},{8,6},{10,8},{12,10},{14,12},{16,14},{18,16},{20... | collective-permute-start | bytes 589832 | tf_op jit(solution)/shard_map/ppermute | solution.py:27
  388.4 6.5 %collective-permute-done.6 = bf16[128,768]{0,1:T(8,128)(2,1)S(1)} collective-permute-done((bf16[128,768]{0,1:T(8,128)(2,1)S(1)}, bf16[128,768]{0,1:T(8,128)(2,1)S(1)}, u32[]{:S(2)}, u32[]{:S(2)}) %collective-permute-start.6) | collective-permute-done | bytes 196640 | tf_op jit(solution)/shard_map/ppermute | solution.py:25
  (373 shorter events, 100.2 us)
Async XLA Ops:
  7.2 45.4 %copy-start = (s32[32,4]{0,1:T(4,128)S(1)}, s32[32,4]{0,1:T(4,128)}, u32[]{:S(2)}) copy-start(s32[32,4]{0,1:T(4,128)} %param.13) | copy-start | bytes 1540
  7.2 97.1 %all-gather.4.cloned.1.call-start = ((), (), s32[]{:S(2)}) async-start(), calls=%async_computation.5 | async-start | bytes 3649536 | tf_op jit(solution)/shard_map/all_gather | solution.py:219
  7.9 181.3 %all-gather.6.cloned.1.call-start = ((), (), s32[]{:S(2)}) async-start(), calls=%async_computation.6 | async-start | bytes 1216512 | tf_op jit(solution)/shard_map/all_gather | solution.py:220
  39.1 45.9 %copy-start.23 = (bf16[1,128,768]{2,1,0:T(8,128)(2,1)S(1)}, bf16[1,128,768]{2,1,0:T(8,128)(2,1)}, u32[]{:S(2)}) copy-start(bf16[1,128,768]{2,1,0:T(8,128)(2,1)} %param.8) | copy-start | bytes 589828
  39.1 45.9 %all-to-all-start.2 = ((bf16[32,24,768]{2,1,0:T(8,128)(2,1)}), bf16[32,24,768]{2,1,0:T(8,128)(2,1)S(1)}, u32[]{:S(2)}, u32[]{:S(2)}) async-start(bf16[32,24,768]{2,1,0:T(8,128)(2,1)} %bitcast.50), calls=%async_computation.2 | async-start | bytes 2359296 | tf_op jit(solution)/shard_map/all_to_all | solution.py:14
  51.8 224.9 %all-gather.8.cloned.1.call-start = ((), (), s32[]{:S(2)}) async-start(), calls=%async_computation.7 | async-start | bytes 3649536 | tf_op jit(solution)/shard_map/all_gather | solution.py:221
  89.0 196.7 %all-to-all-start.3 = ((bf16[8,2,6144]{2,1,0:T(2,128)(2,1)}), bf16[8,2,6144]{2,1,0:T(2,128)(2,1)S(1)}, u32[]{:S(2)}, u32[]{:S(2)}) async-start(bf16[8,2,6144]{2,1,0:T(2,128)(2,1)} %reshape.407), calls=%async_computation.3 | async-start | bytes 393216 | tf_op jit(solution)/shard_map/all_to_all | solution.py:203
  107.0 15.7 %collective-permute-start.1 = (bf16[128,768]{1,0:T(8,128)(2,1)S(1)}, bf16[128,768]{1,0:T(8,128)(2,1)S(1)}, u32[]{:S(2)}, u32[]{:S(2)}) collective-permute-start(bf16[128,768]{1,0:T(8,128)(2,1)S(1)} %get-tuple-element.28), channel_id=1, source_target_pairs={{2,0},{4,2},{6,4},{8,6},{10,8},{12,10},{14,12},{16,14},{18,16},{20... | collective-permute-start | bytes 589832 | tf_op jit(solution)/shard_map/ppermute | solution.py:27
  111.9 10.9 %collective-permute-start = (bf16[128,768]{1,0:T(8,128)(2,1)S(1)}, bf16[128,768]{1,0:T(8,128)(2,1)S(1)}, u32[]{:S(2)}, u32[]{:S(2)}) collective-permute-start(bf16[128,768]{1,0:T(8,128)(2,1)S(1)} %get-tuple-element.28), channel_id=1, source_target_pairs={{0,2},{2,4},{4,6},{6,8},{8,10},{10,12},{12,14},{14,16},{16,18},{18... | collective-permute-start | bytes 589832 | tf_op jit(solution)/shard_map/ppermute | solution.py:25
  113.8 9.3 %collective-permute-start.3 = (bf16[128,768]{1,0:T(8,128)(2,1)S(1)}, bf16[128,768]{1,0:T(8,128)(2,1)S(1)}, u32[]{:S(2)}, u32[]{:S(2)}) collective-permute-start(bf16[128,768]{1,0:T(8,128)(2,1)S(1)} %get-tuple-element.27), channel_id=1, source_target_pairs={{2,0},{4,2},{6,4},{8,6},{10,8},{12,10},{14,12},{16,14},{18,16},{20... | collective-permute-start | bytes 589832 | tf_op jit(solution)/shard_map/ppermute | solution.py:27
  119.8 9.7 %collective-permute-start.2 = (bf16[128,768]{1,0:T(8,128)(2,1)S(1)}, bf16[128,768]{1,0:T(8,128)(2,1)S(1)}, u32[]{:S(2)}, u32[]{:S(2)}) collective-permute-start(bf16[128,768]{1,0:T(8,128)(2,1)S(1)} %get-tuple-element.27), channel_id=1, source_target_pairs={{0,2},{2,4},{4,6},{6,8},{8,10},{10,12},{12,14},{14,16},{16,18},{18... | collective-permute-start | bytes 589832 | tf_op jit(solution)/shard_map/ppermute | solution.py:25
  129.8 164.9 %copy-start.21 = (bf16[384,128]{0,1:T(8,128)(2,1)}, bf16[384,128]{0,1:T(8,128)(2,1)S(1)}, u32[]{:S(2)}) copy-start(bf16[384,128]{0,1:T(8,128)(2,1)S(1)} %copy.186) | copy-start | bytes 294916
  130.1 166.1 %copy-start.19 = (bf16[384,128]{0,1:T(8,128)(2,1)}, bf16[384,128]{0,1:T(8,128)(2,1)S(1)}, u32[]{:S(2)}) copy-start(bf16[384,128]{0,1:T(8,128)(2,1)S(1)} %copy.189) | copy-start | bytes 294916
  130.6 211.1 %copy-start.14 = (bf16[384,128]{0,1:T(8,128)(2,1)}, bf16[384,128]{0,1:T(8,128)(2,1)S(1)}, u32[]{:S(2)}) copy-start(bf16[384,128]{0,1:T(8,128)(2,1)S(1)} %copy.195) | copy-start | bytes 294916
  130.9 212.0 %copy-start.12 = (bf16[384,128]{0,1:T(8,128)(2,1)}, bf16[384,128]{0,1:T(8,128)(2,1)S(1)}, u32[]{:S(2)}) copy-start(bf16[384,128]{0,1:T(8,128)(2,1)S(1)} %copy.198) | copy-start | bytes 294916
  135.0 56.0 %copy-start.33 = (f32[2,128,384]{2,1,0:T(8,128)}, f32[2,128,384]{2,1,0:T(8,128)S(1)}, u32[]{:S(2)}) copy-start(f32[2,128,384]{2,1,0:T(8,128)S(1)} %fusion.21) | copy-start | bytes 1179652
  191.0 88.5 %copy-start.5 = (f32[128,768]{1,0:T(8,128)}, f32[128,768]{1,0:T(8,128)S(1)}, u32[]{:S(2)}) copy-start(f32[128,768]{1,0:T(8,128)S(1)} %get-tuple-element.40) | copy-start | bytes 1179652
  285.7 22.1 %all-to-all-start = ((bf16[8,2,18432]{2,1,0:T(2,128)(2,1)}), bf16[8,2,18432]{2,1,0:T(2,128)(2,1)S(1)}, u32[]{:S(2)}, u32[]{:S(2)}) async-start(bf16[8,2,18432]{2,1,0:T(2,128)(2,1)} %reshape.405), calls=%async_computation | async-start | bytes 1179648 | tf_op jit(solution)/shard_map/all_to_all | solution.py:203
  323.1 13.1 %all-to-all-start.1 = ((bf16[8,16,768]{2,1,0:T(8,128)(2,1)}), bf16[8,16,768]{2,1,0:T(8,128)(2,1)S(1)}, u32[]{:S(2)}, u32[]{:S(2)}) async-start(bf16[8,16,768]{2,1,0:T(8,128)(2,1)} %reshape.352), calls=%async_computation.1 | async-start | bytes 393216 | tf_op jit(solution)/shard_map/all_to_all | solution.py:207
  336.2 18.2 %all-to-all-start.4 = ((bf16[8,16,2304]{2,1,0:T(8,128)(2,1)}), bf16[8,16,2304]{2,1,0:T(8,128)(2,1)}, u32[]{:S(2)}, u32[]{:S(2)}) async-start(bf16[8,16,2304]{2,1,0:T(8,128)(2,1)} %pad_maximum_fusion.2), calls=%async_computation.4 | async-start | bytes 1179648 | tf_op jit(solution)/shard_map/all_to_all | solution.py:207
  373.1 14.1 %collective-permute-start.5 = (bf16[128,768]{0,1:T(8,128)(2,1)S(1)}, bf16[128,768]{0,1:T(8,128)(2,1)S(1)}, u32[]{:S(2)}, u32[]{:S(2)}) collective-permute-start(bf16[128,768]{0,1:T(8,128)(2,1)S(1)} %get-tuple-element.5), channel_id=1, source_target_pairs={{2,0},{4,2},{6,4},{8,6},{10,8},{12,10},{14,12},{16,14},{18,16},{20... | collective-permute-start | bytes 589832 | tf_op jit(solution)/shard_map/ppermute | solution.py:27
  376.7 10.8 %collective-permute-start.4 = (bf16[128,768]{0,1:T(8,128)(2,1)S(1)}, bf16[128,768]{0,1:T(8,128)(2,1)S(1)}, u32[]{:S(2)}, u32[]{:S(2)}) collective-permute-start(bf16[128,768]{0,1:T(8,128)(2,1)S(1)} %get-tuple-element.4), channel_id=1, source_target_pairs={{0,2},{2,4},{4,6},{6,8},{8,10},{10,12},{12,14},{14,16},{16,18},{18... | collective-permute-start | bytes 589832 | tf_op jit(solution)/shard_map/ppermute | solution.py:25
  379.2 9.2 %collective-permute-start.7 = (bf16[128,768]{0,1:T(8,128)(2,1)S(1)}, bf16[128,768]{0,1:T(8,128)(2,1)S(1)}, u32[]{:S(2)}, u32[]{:S(2)}) collective-permute-start(bf16[128,768]{0,1:T(8,128)(2,1)S(1)} %get-tuple-element.3), channel_id=1, source_target_pairs={{2,0},{4,2},{6,4},{8,6},{10,8},{12,10},{14,12},{16,14},{18,16},{20... | collective-permute-start | bytes 589832 | tf_op jit(solution)/shard_map/ppermute | solution.py:27
  385.2 9.7 %collective-permute-start.6 = (bf16[128,768]{0,1:T(8,128)(2,1)S(1)}, bf16[128,768]{0,1:T(8,128)(2,1)S(1)}, u32[]{:S(2)}, u32[]{:S(2)}) collective-permute-start(bf16[128,768]{0,1:T(8,128)(2,1)S(1)} %get-tuple-element.2), channel_id=1, source_target_pairs={{0,2},{2,4},{4,6},{6,8},{8,10},{10,12},{12,14},{14,16},{16,18},{18... | collective-permute-start | bytes 589832 | tf_op jit(solution)/shard_map/ppermute | solution.py:25
  (76 other events, 274.3 us)
Sparse Core Ops, SparseCore 0:
  11.2 93.0 all-gather.3
  107.5 81.6 all-gather.5
  192.4 84.2 all-gather.7
